TPU v7x, 32 devices: a whole 2x2x4 slice. The times are simulated.
32 devices in a mesh: band: 16 (over z, x, core), chan: 2 (over y).
Axes of the slice: x: 2, y: 2, z: 4, core: 2. Of those that a mesh axis runs over, the one named last changes fastest.
Arguments:
- features: bfloat16 [256, 64, 1024], P('chan', 'band'), may hold values from -6 to 6
- depth_kernel: bfloat16 [3, 9, 256], P(None, None, 'chan'), may hold values from -2 to 2
- pointwise: bfloat16 [4, 256, 256], P(None, 'chan'), may hold values from -0.25 to 0.25
- cotangent: bfloat16 [256, 64, 1024], P('chan', 'band'), may hold values from -6 to 6
Outputs:
- output: bfloat16 [256, 64, 1024], P('chan', 'band')
- grad_input: float32 [256, 64, 1024], P('chan', 'band')
- grad_depth: float32 [3, 9, 256], P(None, None, 'chan')
- grad_point: float32 [4, 256, 256], P(None, 'chan')
All inputs are finite; a program needn't handle non-finite values.
Results may differ from a plain program's by a relative error of at most 0.0057.
Values may be sent and summed in bfloat16 or wider, within the bound.
No kernel may reach another device: no remote copies, remote signals or barrier semaphores. Data moves between devices by JAX's collectives and lax.ppermute only.
A program may use at most 128 MiB of HBM per device.

v0:
```python
import jax
import jax.numpy as jnp
from jax import lax
from jax.sharding import PartitionSpec as P

GSCALE = 1024
dilations = (6, 12, 18)


def shifted(block, axis, distance):
    devices = range(lax.axis_size(axis))
    route = [(i - distance, i) for i in devices if i - distance in devices]
    if not route:
        return jnp.zeros_like(block)
    return lax.ppermute(block, axis, route)


def from_device(block, ahead):
    return block if ahead == 0 else shifted(block, "band", -ahead)


def rows_at(field, offset):
    height = field.shape[1]
    ahead, start = divmod(offset, height)
    if start == 0:
        return from_device(field, ahead)
    return jnp.concatenate(
        [from_device(field[:, start:], ahead), from_device(field[:, :start], ahead + 1)], axis=1
    )


def local(features, depth_kernel, pointwise, cotangent):
    kernel = depth_kernel.astype(jnp.float32)
    feat_rows = {0: features}
    for spacing in dilations:
        for side in (-1, 1):
            feat_rows[side * spacing] = rows_at(features, side * spacing)
    feat_rows = {k: v.astype(jnp.float32) for k, v in feat_rows.items()}
    branches = [features]
    for which, spacing in enumerate(dilations):
        total = jnp.zeros(features.shape, jnp.float32)
        for tap_index in range(9):
            row_step = tap_index // 3 - 1
            col_step = tap_index % 3 - 1
            total = total + kernel[which, tap_index][:, None, None] * jnp.roll(
                feat_rows[row_step * spacing], -col_step * spacing, axis=-1
            )
        branches.append(total.astype(jnp.bfloat16))
    stacked = jnp.stack(branches)
    output = lax.psum_scatter(
        jnp.einsum("bchw,bco->ohw", stacked, pointwise, preferred_element_type=jnp.float32).astype(
            jnp.bfloat16
        ),
        "chan",
        scatter_dimension=0,
        tiled=True,
    )
    cot_full = lax.all_gather(cotangent, "chan", axis=0, tiled=True)
    grad_sum = jnp.einsum("bco,ohw->bchw", pointwise, cot_full, preferred_element_type=jnp.float32)
    point_local = jnp.einsum("bchw,ohw->bco", stacked, cot_full, preferred_element_type=jnp.float32)
    grad_branches = grad_sum.astype(jnp.bfloat16)
    grad_input = grad_branches[0].astype(jnp.float32)
    depth_rows = []
    for which, spacing in enumerate(dilations):
        grad_field = grad_branches[which + 1]
        grad_f = grad_field.astype(jnp.float32)
        grad_rows = {0: grad_f}
        for side in (-1, 1):
            grad_rows[side * spacing] = rows_at(grad_field, side * spacing).astype(jnp.float32)
        tap_rows = []
        for tap_index in range(9):
            row_step = tap_index // 3 - 1
            col_step = tap_index % 3 - 1
            grad_input = grad_input + kernel[which, tap_index][:, None, None] * jnp.roll(
                grad_rows[-row_step * spacing], col_step * spacing, axis=-1
            )
            tap_rows.append(
                jnp.sum(
                    grad_f * jnp.roll(feat_rows[row_step * spacing], -col_step * spacing, axis=-1),
                    axis=(1, 2),
                )
            )
        depth_rows.append(jnp.stack(tap_rows))
    depth_local = jnp.stack(depth_rows)
    flat = jnp.concatenate([depth_local.reshape(-1), point_local.reshape(-1)])
    flat = lax.psum(flat, "band")
    depth_total = flat[: depth_local.size].reshape(depth_local.shape)
    point_total = flat[depth_local.size :].reshape(point_local.shape)
    return (output, grad_input, depth_total / GSCALE, point_total / GSCALE)


def solution(mesh):
    return jax.shard_map(
        local,
        mesh=mesh,
        in_specs=(
            P("chan", "band", None),
            P(None, None, "chan"),
            P(None, "chan", None),
            P("chan", "band", None),
        ),
        out_specs=(
            P("chan", "band", None),
            P("chan", "band", None),
            P(None, None, "chan"),
            P(None, "chan", None),
        ),
        check_vma=False,
    )
```

profile of v0, /device:TPU:0, one launch (start us, length us, event | category | flops | bytes accessed | tf_op | source)
XLA Modules:
  0.0 347.8 jit_solution(9047192822826043685)
XLA Ops:
  11.5 5.1 %collective-permute-start.6 = (bf16[128,2,1024]{0,2,1:T(8,128)(2,1)}, bf16[128,2,1024]{0,2,1:T(8,128)(2,1)S(1)}, u32[]{:S(2)}, u32[]{:S(2)}) collective-permute-start(bf16[128,2,1024]{0,2,1:T(8,128)(2,1)} %get-tuple-element.125), channel_id=1, source_target_pairs={{0,10},{2,12},{4,14},{6,16},{8,18},{10,20},{12,22},{14,24},{16,26}... | collective-permute-start | bytes 1572872 | tf_op jit(solution)/shard_map/ppermute | solution.py:15
  17.9 7.0 %collective-permute-start = (bf16[128,2,1024]{0,2,1:T(8,128)(2,1)}, bf16[128,2,1024]{0,2,1:T(8,128)(2,1)}, u32[]{:S(2)}, u32[]{:S(2)}) collective-permute-start(bf16[128,2,1024]{0,2,1:T(8,128)(2,1)} %get-tuple-element.125), channel_id=1, source_target_pairs={{0,4},{2,6},{4,8},{6,10},{8,12},{10,14},{12,16},{14,18},{16,20},{1... | collective-permute-start | bytes 1572872 | tf_op jit(solution)/shard_map/ppermute | solution.py:15
  34.1 7.1 %collective-permute-done.7 = bf16[128,2,1024]{0,2,1:T(8,128)(2,1)S(1)} collective-permute-done((bf16[128,2,1024]{0,2,1:T(8,128)(2,1)}, bf16[128,2,1024]{0,2,1:T(8,128)(2,1)S(1)}, u32[]{:S(2)}, u32[]{:S(2)}) %collective-permute-start.7) | collective-permute-done | bytes 524320 | tf_op jit(solution)/shard_map/ppermute | solution.py:15
  50.4 19.0 %collective-permute-start.4 = (bf16[128,4,1024]{0,2,1:T(8,128)(2,1)S(1)}, bf16[128,4,1024]{0,2,1:T(8,128)(2,1)S(1)}, u32[]{:S(2)}, u32[]{:S(2)}) collective-permute-start(bf16[128,4,1024]{0,2,1:T(8,128)(2,1)S(1)} %copy.35), channel_id=1, source_target_pairs={{0,6},{2,8},{4,10},{6,12},{8,14},{10,16},{12,18},{14,20},{16,22},{... | collective-permute-start | bytes 3145736 | tf_op jit(solution)/shard_map/ppermute | solution.py:15
  74.7 7.1 %fusion.75 = bf16[1,128,4,1024]{1,3,0,2:T(8,128)(2,1)} fusion(f32[128,4,18]{0,2,1:T(8,128)S(1)} %get-tuple-element.90, f32[128,4,1006]{0,2,1:T(8,128)} %get-tuple-element.92, f32[128]{0:T(128)S(1)} %get-tuple-element.128, f32[128]{0:T(128)S(1)} %get-tuple-element.129, f32[128,4,1006]{0,2,1:T(8,128)} %get-tuple-element.91, ...), kind=kLoop, calls=%fused_computation.159 | loop fusion | flops 15204352 | bytes 16781824 | tf_op jit(solution)/shard_map/stack | solution.py:49
  82.0 5.8 %fusion.77 = bf16[1,128,4,1024]{1,3,0,2:T(8,128)(2,1)} fusion(f32[128,4,6]{0,2,1:T(8,128)S(1)} %get-tuple-element.82, f32[128,4,1018]{0,2,1:T(8,128)S(1)} %get-tuple-element.84, f32[128]{0:T(128)} %get-tuple-element.147, f32[128]{0:T(128)} %get-tuple-element.148, f32[128,4,1018]{0,2,1:T(8,128)S(1)} %get-tuple-element.83, ...), kind=kLoop, calls=%fused_computation.161 | loop fusion | flops 15204352 | bytes 16781824 | tf_op jit(solution)/shard_map/stack | solution.py:49
  87.9 9.6 %collective-permute-done.4 = bf16[128,4,1024]{0,2,1:T(8,128)(2,1)S(1)} collective-permute-done((bf16[128,4,1024]{0,2,1:T(8,128)(2,1)S(1)}, bf16[128,4,1024]{0,2,1:T(8,128)(2,1)S(1)}, u32[]{:S(2)}, u32[]{:S(2)}) %collective-permute-start.4) | collective-permute-done | bytes 1048608 | tf_op jit(solution)/shard_map/ppermute | solution.py:15
  101.3 4.3 %fusion.76 = bf16[1,128,4,1024]{1,3,0,2:T(8,128)(2,1)} fusion(f32[128,4,12]{0,2,1:T(8,128)S(1)} %get-tuple-element.118, f32[128,4,1012]{0,2,1:T(8,128)S(1)} %get-tuple-element.120, f32[128]{0:T(128)S(1)} %copy-done.97, bf16[128,4,1024]{0,2,1:T(8,128)(2,1)S(1)} %collective-permute-done.5, f32[128]{0:T(128)S(1)} %copy-done.98, ...), kind=kLoop, calls=%fused_computation.160 | loop fusion | flops 14155776 | bytes 16781824 | tf_op jit(solution)/shard_map/stack | solution.py:49
  105.7 3.0 convolution_convert_fusion
  109.2 5.9 %fusion.47 = (f32[128]{0:T(128)}, f32[128]{0:T(128)}, f32[128]{0:T(128)}, f32[128]{0:T(128)}, f32[128]{0:T(128)}, /*index=5*/f32[128]{0:T(128)}) fusion(f32[128,4,1018]{0,2,1:T(8,128)S(1)} %copy-done.15, f32[128,4,6]{0,2,1:T(8,128)S(1)} %copy-done.84, bf16[4,128,4,1024]{1,3,2,0:T(8,128)(2,1)S(1)} %convolution_convert_fusion, ...), kind=kLoop, calls=%fused_computation.83 | loop fusion | flops 10484992 | bytes 14683136 | tf_op jit(solution)/shard_map/reduce_sum | solution.py:78
  118.5 4.5 %fusion.48 = (f32[128]{0:T(128)}, f32[128]{0:T(128)}, f32[128]{0:T(128)}, f32[128]{0:T(128)}, f32[128]{0:T(128)}, /*index=5*/f32[128]{0:T(128)}, f32[128]{0:T(128)}) fusion(bf16[128,2,1024]{0,2,1:T(8,128)(2,1)S(1)} %copy-done.41, bf16[128,2,1024]{0,2,1:T(8,128)(2,1)} %collective-permute-done.2, bf16[4,128,4,1024]{1,3,2,0:T(8,128)(2,1)S(1)} %convolution_convert_fusion, ...), kind=kLoop, calls=%fused_computation.84 | loop fusion | flops 13630592 | bytes 13635072 | tf_op jit(solution)/shard_map/reduce_sum | solution.py:78
  123.1 4.9 %fusion.45 = (f32[128]{0:T(128)}, f32[128]{0:T(128)}, f32[128]{0:T(128)}, f32[128]{0:T(128)}, f32[128]{0:T(128)}, /*index=5*/f32[128]{0:T(128)}, f32[128]{0:T(128)}, f32[128]{0:T(128)}) fusion(bf16[128,4,1024]{0,2,1:T(8,128)(2,1)S(1)} %copy.35, bf16[4,128,4,1024]{1,3,2,0:T(8,128)(2,1)S(1)} %convolution_convert_fusion, f32[128,4,6]{0,2,1:T(8,128)S(1)} %copy-done.77, ...), kind=kLoop, calls=%fused_computation.81 | loop fusion | flops 13630464 | bytes 13635584 | tf_op jit(solution)/shard_map/reduce_sum | solution.py:78
  130.5 6.4 %fusion.49 = (f32[128]{0:T(128)}, f32[128]{0:T(128)}, f32[128]{0:T(128)}, f32[128]{0:T(128)}, f32[128]{0:T(128)}, /*index=5*/f32[128]{0:T(128)}) fusion(f32[128,4,6]{0,2,1:T(8,128)} %copy-done.78, f32[128,4,1018]{0,2,1:T(8,128)S(1)} %copy-done.13, bf16[4,128,4,1024]{1,3,2,0:T(8,128)(2,1)} %copy-done.2, f32[128,4,18]{0,2,1:T(8,128)} %copy-done.57, ...), kind=kLoop, calls=%fused_computation.85 | loop fusion | flops 11009280 | bytes 13634560 | tf_op jit(solution)/shard_map/reduce_sum | solution.py:78
  142.4 3.1 bitcast_convert_fusion
  145.5 3.0 copy.56
  148.5 3.9 %fusion.84 = (f32[128,4,1024]{0,2,1:T(8,128)S(1)}, f32[128,4,1024]{0,2,1:T(8,128)S(1)}, f32[128,4,1024]{0,2,1:T(8,128)S(1)}, bf16[128,4,1024]{0,2,1:T(8,128)(2,1...) fusion(bf16[4,128,4,1024]{1,3,2,0:T(8,128)(2,1)} %copy-done.2), kind=kLoop, calls=%fused_computation.199 | loop fusion | flops 1572864 | bytes 12582912 | tf_op jit(solution)/shard_map/convert_element_type | solution.py:66
  153.5 20.2 %collective-permute-start.18 = (bf16[128,2,1024]{0,2,1:T(8,128)(2,1)}, bf16[128,2,1024]{0,2,1:T(8,128)(2,1)S(1)}, u32[]{:S(2)}, u32[]{:S(2)}) collective-permute-start(bf16[128,2,1024]{0,2,1:T(8,128)(2,1)} %get-tuple-element.93), channel_id=1, source_target_pairs={{0,10},{2,12},{4,14},{6,16},{8,18},{10,20},{12,22},{14,24},{16,26}... | collective-permute-start | bytes 1572872 | tf_op jit(solution)/shard_map/ppermute | solution.py:15
  175.0 5.6 %collective-permute-start.19 = (bf16[128,2,1024]{0,2,1:T(8,128)(2,1)}, bf16[128,2,1024]{0,2,1:T(8,128)(2,1)S(1)}, u32[]{:S(2)}, u32[]{:S(2)}) collective-permute-start(bf16[128,2,1024]{0,2,1:T(8,128)(2,1)} %get-tuple-element.94), channel_id=1, source_target_pairs={{0,8},{2,10},{4,12},{6,14},{8,16},{10,18},{12,20},{14,22},{16,24},... | collective-permute-start | bytes 1572872 | tf_op jit(solution)/shard_map/ppermute | solution.py:15
  192.9 66.5 %all-reduce.2.cloned.1.call-done = f32[134528]{0:T(1024)} async-done(((f32[134528]{0:T(1024)}), f32[134528]{0:T(1024)}) %all-reduce.2.cloned.1.call-update) | async-done | bytes 538128 | tf_op jit(solution)/shard_map/psum | solution.py:86
  264.1 3.1 collective-permute-start.13
  271.0 6.0 %collective-permute-start.15 = (bf16[128,4,1024]{0,2,1:T(8,128)(2,1)S(1)}, bf16[128,4,1024]{0,2,1:T(8,128)(2,1)S(1)}, u32[]{:S(2)}, u32[]{:S(2)}) collective-permute-start(bf16[128,4,1024]{0,2,1:T(8,128)(2,1)S(1)} %copy-done.54), channel_id=1, source_target_pairs={{0,6},{2,8},{4,10},{6,12},{8,14},{10,16},{12,18},{14,20},{16,22},{... | collective-permute-start | bytes 3145736 | tf_op jit(solution)/shard_map/ppermute | solution.py:15
  280.7 4.8 %collective-permute-done.11 = bf16[128,2,1024]{0,2,1:T(8,128)(2,1)S(1)} collective-permute-done((bf16[128,2,1024]{0,2,1:T(8,128)(2,1)}, bf16[128,2,1024]{0,2,1:T(8,128)(2,1)S(1)}, u32[]{:S(2)}, u32[]{:S(2)}) %collective-permute-start.11) | collective-permute-done | bytes 524320 | tf_op jit(solution)/shard_map/ppermute | solution.py:15
  288.3 24.8 %collective-permute-done.15 = bf16[128,4,1024]{0,2,1:T(8,128)(2,1)S(1)} collective-permute-done((bf16[128,4,1024]{0,2,1:T(8,128)(2,1)S(1)}, bf16[128,4,1024]{0,2,1:T(8,128)(2,1)S(1)}, u32[]{:S(2)}, u32[]{:S(2)}) %collective-permute-start.15) | collective-permute-done | bytes 1048608 | tf_op jit(solution)/shard_map/ppermute | solution.py:15
  320.4 15.6 %fusion.40 = f32[128,4,1024]{0,2,1:T(8,128)S(1)} fusion(f32[128,4,6]{0,2,1:T(8,128)S(1)} %get-tuple-element.74, f32[128,4,1018]{0,2,1:T(8,128)S(1)} %get-tuple-element.76, f32[128,4,1018]{0,2,1:T(8,128)S(1)} %get-tuple-element.75, f32[128,4,6]{0,2,1:T(8,128)S(1)} %get-tuple-element.73, f32[128,4,6]{0,2,1:T(8,128)S(1)} %get-tuple-element.70, ...), kind=kLoop, calls=%fused_computation.76 | loop fusion | flops 45088768 | bytes 50345472 | tf_op jit(solution)/shard_map/add | solution.py:74
  (317 shorter events, 86.1 us)
Async XLA Ops:
  7.2 98.4 %copy-start = (bf16[4,128,256]{2,1,0:T(8,128)(2,1)S(1)}, bf16[4,128,256]{2,1,0:T(8,128)(2,1)}, u32[]{:S(2)}) copy-start(bf16[4,128,256]{2,1,0:T(8,128)(2,1)} %param.6) | copy-start | bytes 786436
  7.2 98.4 %all-gather.2.cloned.1.call-start = ((), (), s32[]{:S(2)}) async-start(), calls=%async_computation.1 | async-start | bytes 3145728 | tf_op jit(solution)/shard_map/all_gather | solution.py:58
  10.2 34.8 %collective-permute-start.8 = (bf16[128,2,1024]{0,2,1:T(8,128)(2,1)}, bf16[128,2,1024]{0,2,1:T(8,128)(2,1)S(1)}, u32[]{:S(2)}, u32[]{:S(2)}) collective-permute-start(bf16[128,2,1024]{0,2,1:T(8,128)(2,1)} %get-tuple-element.125), channel_id=1, source_target_pairs={{8,0},{10,2},{12,4},{14,6},{16,8},{18,10},{20,12},{22,14},{24,16},... | collective-permute-start | bytes 1572872 | tf_op jit(solution)/shard_map/ppermute | solution.py:15
  11.5 21.3 %collective-permute-start.6 = (bf16[128,2,1024]{0,2,1:T(8,128)(2,1)}, bf16[128,2,1024]{0,2,1:T(8,128)(2,1)S(1)}, u32[]{:S(2)}, u32[]{:S(2)}) collective-permute-start(bf16[128,2,1024]{0,2,1:T(8,128)(2,1)} %get-tuple-element.125), channel_id=1, source_target_pairs={{0,10},{2,12},{4,14},{6,16},{8,18},{10,20},{12,22},{14,24},{16,26}... | collective-permute-start | bytes 1572872 | tf_op jit(solution)/shard_map/ppermute | solution.py:15
  16.6 33.8 %collective-permute-start.2 = (bf16[128,2,1024]{0,2,1:T(8,128)(2,1)}, bf16[128,2,1024]{0,2,1:T(8,128)(2,1)}, u32[]{:S(2)}, u32[]{:S(2)}) collective-permute-start(bf16[128,2,1024]{0,2,1:T(8,128)(2,1)} %get-tuple-element.125), channel_id=1, source_target_pairs={{2,0},{4,2},{6,4},{8,6},{10,8},{12,10},{14,12},{16,14},{18,16},{20... | collective-permute-start | bytes 1572872 | tf_op jit(solution)/shard_map/ppermute | solution.py:15
  17.9 53.2 %collective-permute-start = (bf16[128,2,1024]{0,2,1:T(8,128)(2,1)}, bf16[128,2,1024]{0,2,1:T(8,128)(2,1)}, u32[]{:S(2)}, u32[]{:S(2)}) collective-permute-start(bf16[128,2,1024]{0,2,1:T(8,128)(2,1)} %get-tuple-element.125), channel_id=1, source_target_pairs={{0,4},{2,6},{4,8},{6,10},{8,12},{10,14},{12,16},{14,18},{16,20},{1... | collective-permute-start | bytes 1572872 | tf_op jit(solution)/shard_map/ppermute | solution.py:15
  26.3 233.1 %all-reduce.2.cloned.1.call-start = ((), (), s32[]{:S(2)}) async-start(), calls=%async_computation.2 | async-start | bytes 1081344 | tf_op jit(solution)/shard_map/psum | solution.py:86
  26.3 14.9 %collective-permute-start.7 = (bf16[128,2,1024]{0,2,1:T(8,128)(2,1)}, bf16[128,2,1024]{0,2,1:T(8,128)(2,1)S(1)}, u32[]{:S(2)}, u32[]{:S(2)}) collective-permute-start(bf16[128,2,1024]{0,2,1:T(8,128)(2,1)} %get-tuple-element.126), channel_id=1, source_target_pairs={{0,8},{2,10},{4,12},{6,14},{8,16},{10,18},{12,20},{14,22},{16,24},... | collective-permute-start | bytes 1572872 | tf_op jit(solution)/shard_map/ppermute | solution.py:15
  32.8 13.9 %collective-permute-start.9 = (bf16[128,2,1024]{0,2,1:T(8,128)(2,1)}, bf16[128,2,1024]{0,2,1:T(8,128)(2,1)S(1)}, u32[]{:S(2)}, u32[]{:S(2)}) collective-permute-start(bf16[128,2,1024]{0,2,1:T(8,128)(2,1)} %get-tuple-element.126), channel_id=1, source_target_pairs={{10,0},{12,2},{14,4},{16,6},{18,8},{20,10},{22,12},{24,14},{26,16}... | collective-permute-start | bytes 1572872 | tf_op jit(solution)/shard_map/ppermute | solution.py:15
  41.2 28.2 %collective-permute-start.3 = (bf16[128,2,1024]{0,2,1:T(8,128)(2,1)}, bf16[128,2,1024]{0,2,1:T(8,128)(2,1)S(1)}, u32[]{:S(2)}, u32[]{:S(2)}) collective-permute-start(bf16[128,2,1024]{0,2,1:T(8,128)(2,1)} %get-tuple-element.126), channel_id=1, source_target_pairs={{4,0},{6,2},{8,4},{10,6},{12,8},{14,10},{16,12},{18,14},{20,16},{2... | collective-permute-start | bytes 1572872 | tf_op jit(solution)/shard_map/ppermute | solution.py:15
  45.0 26.1 %collective-permute-start.1 = (bf16[128,2,1024]{0,2,1:T(8,128)(2,1)}, bf16[128,2,1024]{0,2,1:T(8,128)(2,1)S(1)}, u32[]{:S(2)}, u32[]{:S(2)}) collective-permute-start(bf16[128,2,1024]{0,2,1:T(8,128)(2,1)} %get-tuple-element.126), channel_id=1, source_target_pairs={{0,2},{2,4},{4,6},{6,8},{8,10},{10,12},{12,14},{14,16},{16,18},{18... | collective-permute-start | bytes 1572872 | tf_op jit(solution)/shard_map/ppermute | solution.py:15
  46.7 41.2 %collective-permute-start.5 = (bf16[128,4,1024]{0,2,1:T(8,128)(2,1)S(1)}, bf16[128,4,1024]{0,2,1:T(8,128)(2,1)S(1)}, u32[]{:S(2)}, u32[]{:S(2)}) collective-permute-start(bf16[128,4,1024]{0,2,1:T(8,128)(2,1)S(1)} %copy.35), channel_id=1, source_target_pairs={{6,0},{8,2},{10,4},{12,6},{14,8},{16,10},{18,12},{20,14},{22,16},{... | collective-permute-start | bytes 3145736 | tf_op jit(solution)/shard_map/ppermute | solution.py:15
  50.4 47.1 %collective-permute-start.4 = (bf16[128,4,1024]{0,2,1:T(8,128)(2,1)S(1)}, bf16[128,4,1024]{0,2,1:T(8,128)(2,1)S(1)}, u32[]{:S(2)}, u32[]{:S(2)}) collective-permute-start(bf16[128,4,1024]{0,2,1:T(8,128)(2,1)S(1)} %copy.35), channel_id=1, source_target_pairs={{0,6},{2,8},{4,10},{6,12},{8,14},{10,16},{12,18},{14,20},{16,22},{... | collective-permute-start | bytes 3145736 | tf_op jit(solution)/shard_map/ppermute | solution.py:15
  142.3 195.6 %reduce-scatter.4.cloned.1.call-start = ((), (), s32[]{:S(2)}) async-start(), calls=%async_computation.3 | async-start | bytes 3145728
  153.5 116.2 %collective-permute-start.18 = (bf16[128,2,1024]{0,2,1:T(8,128)(2,1)}, bf16[128,2,1024]{0,2,1:T(8,128)(2,1)S(1)}, u32[]{:S(2)}, u32[]{:S(2)}) collective-permute-start(bf16[128,2,1024]{0,2,1:T(8,128)(2,1)} %get-tuple-element.93), channel_id=1, source_target_pairs={{0,10},{2,12},{4,14},{6,16},{8,18},{10,20},{12,22},{14,24},{16,26}... | collective-permute-start | bytes 1572872 | tf_op jit(solution)/shard_map/ppermute | solution.py:15
  173.7 89.1 %collective-permute-start.16 = (bf16[128,2,1024]{0,2,1:T(8,128)(2,1)}, bf16[128,2,1024]{0,2,1:T(8,128)(2,1)S(1)}, u32[]{:S(2)}, u32[]{:S(2)}) collective-permute-start(bf16[128,2,1024]{0,2,1:T(8,128)(2,1)} %get-tuple-element.93), channel_id=1, source_target_pairs={{8,0},{10,2},{12,4},{14,6},{16,8},{18,10},{20,12},{22,14},{24,16},... | collective-permute-start | bytes 1572872 | tf_op jit(solution)/shard_map/ppermute | solution.py:15
  175.0 96.0 %collective-permute-start.19 = (bf16[128,2,1024]{0,2,1:T(8,128)(2,1)}, bf16[128,2,1024]{0,2,1:T(8,128)(2,1)S(1)}, u32[]{:S(2)}, u32[]{:S(2)}) collective-permute-start(bf16[128,2,1024]{0,2,1:T(8,128)(2,1)} %get-tuple-element.94), channel_id=1, source_target_pairs={{0,8},{2,10},{4,12},{6,14},{8,16},{10,18},{12,20},{14,22},{16,24},... | collective-permute-start | bytes 1572872 | tf_op jit(solution)/shard_map/ppermute | solution.py:15
  180.6 83.5 %collective-permute-start.17 = (bf16[128,2,1024]{0,2,1:T(8,128)(2,1)}, bf16[128,2,1024]{0,2,1:T(8,128)(2,1)S(1)}, u32[]{:S(2)}, u32[]{:S(2)}) collective-permute-start(bf16[128,2,1024]{0,2,1:T(8,128)(2,1)} %get-tuple-element.94), channel_id=1, source_target_pairs={{10,0},{12,2},{14,4},{16,6},{18,8},{20,10},{22,12},{24,14},{26,16}... | collective-permute-start | bytes 1572872 | tf_op jit(solution)/shard_map/ppermute | solution.py:15
  190.0 95.7 %collective-permute-start.12 = (bf16[128,2,1024]{0,2,1:T(8,128)(2,1)}, bf16[128,2,1024]{0,2,1:T(8,128)(2,1)}, u32[]{:S(2)}, u32[]{:S(2)}) collective-permute-start(bf16[128,2,1024]{0,2,1:T(8,128)(2,1)} %get-tuple-element.103), channel_id=1, source_target_pairs={{0,4},{2,6},{4,8},{6,10},{8,12},{10,14},{12,16},{14,18},{16,20},{1... | collective-permute-start | bytes 1572872 | tf_op jit(solution)/shard_map/ppermute | solution.py:15
  262.8 16.6 %collective-permute-start.10 = (bf16[128,2,1024]{0,2,1:T(8,128)(2,1)}, bf16[128,2,1024]{0,2,1:T(8,128)(2,1)S(1)}, u32[]{:S(2)}, u32[]{:S(2)}) collective-permute-start(bf16[128,2,1024]{0,2,1:T(8,128)(2,1)} %get-tuple-element.103), channel_id=1, source_target_pairs={{2,0},{4,2},{6,4},{8,6},{10,8},{12,10},{14,12},{16,14},{18,16},{20... | collective-permute-start | bytes 1572872 | tf_op jit(solution)/shard_map/ppermute | solution.py:15
  264.1 21.6 %collective-permute-start.13 = (bf16[128,2,1024]{0,2,1:T(8,128)(2,1)}, bf16[128,2,1024]{0,2,1:T(8,128)(2,1)S(1)}, u32[]{:S(2)}, u32[]{:S(2)}) collective-permute-start(bf16[128,2,1024]{0,2,1:T(8,128)(2,1)} %get-tuple-element.104), channel_id=1, source_target_pairs={{0,2},{2,4},{4,6},{6,8},{8,10},{10,12},{12,14},{14,16},{16,18},{18... | collective-permute-start | bytes 1572872 | tf_op jit(solution)/shard_map/ppermute | solution.py:15
  269.7 15.8 %collective-permute-start.11 = (bf16[128,2,1024]{0,2,1:T(8,128)(2,1)}, bf16[128,2,1024]{0,2,1:T(8,128)(2,1)S(1)}, u32[]{:S(2)}, u32[]{:S(2)}) collective-permute-start(bf16[128,2,1024]{0,2,1:T(8,128)(2,1)} %get-tuple-element.104), channel_id=1, source_target_pairs={{4,0},{6,2},{8,4},{10,6},{12,8},{14,10},{16,12},{18,14},{20,16},{2... | collective-permute-start | bytes 1572872 | tf_op jit(solution)/shard_map/ppermute | solution.py:15
  271.0 42.1 %collective-permute-start.15 = (bf16[128,4,1024]{0,2,1:T(8,128)(2,1)S(1)}, bf16[128,4,1024]{0,2,1:T(8,128)(2,1)S(1)}, u32[]{:S(2)}, u32[]{:S(2)}) collective-permute-start(bf16[128,4,1024]{0,2,1:T(8,128)(2,1)S(1)} %copy-done.54), channel_id=1, source_target_pairs={{0,6},{2,8},{4,10},{6,12},{8,14},{10,16},{12,18},{14,20},{16,22},{... | collective-permute-start | bytes 3145736 | tf_op jit(solution)/shard_map/ppermute | solution.py:15
  279.4 33.7 %collective-permute-start.14 = (bf16[128,4,1024]{0,2,1:T(8,128)(2,1)S(1)}, bf16[128,4,1024]{0,2,1:T(8,128)(2,1)S(1)}, u32[]{:S(2)}, u32[]{:S(2)}) collective-permute-start(bf16[128,4,1024]{0,2,1:T(8,128)(2,1)S(1)} %copy-done.54), channel_id=1, source_target_pairs={{6,0},{8,2},{10,4},{12,6},{14,8},{16,10},{18,12},{20,14},{22,16},{... | collective-permute-start | bytes 3145736 | tf_op jit(solution)/shard_map/ppermute | solution.py:15
  (105 other events, 1523.1 us)
Sparse Core Ops, SparseCore 0:
  26.4 32.4 all-gather.1
  142.4 116.8 all-reduce.1
  261.6 32.2 reduce-scatter.3
where the time goes:
time: 349 us; the launch traced here: 348 us
  waiting for transfers between devices  113 us (32%)
  starting transfers between devices  86.2 us (25%)
  other arithmetic  67.8 us (19%)
  local copies, waits for them, and re-layouts  58 us (17%)
  between operations  15.4 us (4%)
  matrix products  7.47 us (2%)
    ppermute x20, starting transfers between devices, shifted(): return lax.ppermute(block, axis, route)  86.1 us
    psum x1, waiting for transfers between devices, local(): flat = lax.psum(flat, 'band')  66.5 us
    ppermute x20, waiting for transfers between devices, shifted(): return lax.ppermute(block, axis, route)  46.3 us
    reduce_sum x4, other arithmetic, local(): jnp.sum(grad_f * jnp.roll(feat_rows[row_step * spacing], -col_step * spac...  21.7 us
    unnamed x220, local copies, waits for them, and re-layouts  20.7 us
    slice x18, local copies, waits for them, and re-layouts, local(): jnp.roll(grad_rows[-row_step * spacing], col_step * spacing, axis=-1)  17.5 us
    another operation x3, other arithmetic, local(): stacked = jnp.stack(branches)  17.2 us
    add x1, other arithmetic, local(): grad_input + kernel[which, tap_index][:, None, None] * jnp.roll(grad_rows...  15.6 us
  transfers between devices with their start and end apart: 23, of which 5 were waited for; matrix products, arithmetic and copies ran while one was open for 24% of the time, Pallas kernels for 0%

commit v1 on v0

--- a/solution.py
+++ b/solution.py
@@ -83,7 +83,8 @@
         depth_rows.append(jnp.stack(tap_rows))
     depth_local = jnp.stack(depth_rows)
     flat = jnp.concatenate([depth_local.reshape(-1), point_local.reshape(-1)])
-    flat = lax.psum(flat, "band")
+    current_arr = lax.all_gather(flat, "band")
+    flat = jnp.sum(current_arr, 0)
     depth_total = flat[: depth_local.size].reshape(depth_local.shape)
     point_total = flat[depth_local.size :].reshape(point_local.shape)
     return (output, grad_input, depth_total / GSCALE, point_total / GSCALE)

time: 349 us -> 366 us (1.049)
  the two profiles are of different devices: /device:TPU:0 before, /device:TPU:18 now
where the time goes in v1:
time: 366 us; the launch traced here: 365 us
  waiting for transfers between devices  112 us (31%)
  other arithmetic  97.2 us (27%)
  starting transfers between devices  78.2 us (21%)
  local copies, waits for them, and re-layouts  54.1 us (15%)
  between operations  15.8 us (4%)
  matrix products  7.72 us (2%)
    ppermute x20, waiting for transfers between devices, shifted(): return lax.ppermute(block, axis, route)  112 us
    ppermute x20, starting transfers between devices, shifted(): return lax.ppermute(block, axis, route)  77.9 us
    reduce_sum x1, other arithmetic, local(): flat = jnp.sum(current_arr, 0)  41.2 us
    unnamed x251, local copies, waits for them, and re-layouts  29.4 us
    reduce_sum x4, other arithmetic, local(): jnp.sum(grad_f * jnp.roll(feat_rows[row_step * spacing], -col_step * spac...  17.3 us
    add x1, other arithmetic, local(): grad_input + kernel[which, tap_index][:, None, None] * jnp.roll(grad_rows...  15.8 us
    another operation x3, other arithmetic, local(): stacked = jnp.stack(branches)  14.5 us
    slice x18, local copies, waits for them, and re-layouts, local(): jnp.roll(grad_rows[-row_step * spacing], col_step * spacing, axis=-1)  13.9 us
  transfers between devices with their start and end apart: 23, of which 8 were waited for; matrix products, arithmetic and copies ran while one was open for 28% of the time, Pallas kernels for 0%

profile of v1, /device:TPU:18, one launch (start us, length us, event | category | flops | bytes accessed | tf_op | source)
XLA Modules:
  0.0 364.7 jit_solution(14777609560756283929)
XLA Ops:
  12.7 3.5 collective-permute-start.6
  16.1 3.9 %collective-permute-start.2 = (bf16[128,2,1024]{0,2,1:T(8,128)(2,1)}, bf16[128,2,1024]{0,2,1:T(8,128)(2,1)}, u32[]{:S(2)}, u32[]{:S(2)}) collective-permute-start(bf16[128,2,1024]{0,2,1:T(8,128)(2,1)} %get-tuple-element.125), channel_id=1, source_target_pairs={{2,0},{4,2},{6,4},{8,6},{10,8},{12,10},{14,12},{16,14},{18,16},{20... | collective-permute-start | bytes 1572872 | tf_op jit(solution)/shard_map/ppermute | solution.py:15
  32.3 27.8 %collective-permute-done.7 = bf16[128,2,1024]{0,2,1:T(8,128)(2,1)S(1)} collective-permute-done((bf16[128,2,1024]{0,2,1:T(8,128)(2,1)}, bf16[128,2,1024]{0,2,1:T(8,128)(2,1)S(1)}, u32[]{:S(2)}, u32[]{:S(2)}) %collective-permute-start.7) | collective-permute-done | bytes 524320 | tf_op jit(solution)/shard_map/ppermute | solution.py:15
  65.6 3.3 collective-permute-start.1
  68.9 2.8 collective-permute-start.5
  75.2 3.9 %collective-permute-start.4 = (bf16[128,4,1024]{0,2,1:T(8,128)(2,1)S(1)}, bf16[128,4,1024]{0,2,1:T(8,128)(2,1)S(1)}, u32[]{:S(2)}, u32[]{:S(2)}) collective-permute-start(bf16[128,4,1024]{0,2,1:T(8,128)(2,1)S(1)} %copy.35), channel_id=1, source_target_pairs={{0,6},{2,8},{4,10},{6,12},{8,14},{10,16},{12,18},{14,20},{16,22},{... | collective-permute-start | bytes 3145736 | tf_op jit(solution)/shard_map/ppermute | solution.py:15
  81.4 14.9 %collective-permute-done.1 = bf16[128,2,1024]{0,2,1:T(8,128)(2,1)S(1)} collective-permute-done((bf16[128,2,1024]{0,2,1:T(8,128)(2,1)}, bf16[128,2,1024]{0,2,1:T(8,128)(2,1)S(1)}, u32[]{:S(2)}, u32[]{:S(2)}) %collective-permute-start.1) | collective-permute-done | bytes 524320 | tf_op jit(solution)/shard_map/ppermute | solution.py:15
  99.3 7.3 %fusion.75 = bf16[1,128,4,1024]{1,3,0,2:T(8,128)(2,1)} fusion(f32[128,4,18]{0,2,1:T(8,128)S(1)} %get-tuple-element.90, f32[128,4,1006]{0,2,1:T(8,128)} %get-tuple-element.92, f32[128]{0:T(128)S(1)} %get-tuple-element.128, f32[128]{0:T(128)S(1)} %get-tuple-element.129, f32[128,4,1006]{0,2,1:T(8,128)} %get-tuple-element.91, ...), kind=kLoop, calls=%fused_computation.159 | loop fusion | flops 15204352 | bytes 16781824 | tf_op jit(solution)/shard_map/stack | solution.py:49
  106.7 5.0 %fusion.77 = bf16[1,128,4,1024]{1,3,0,2:T(8,128)(2,1)S(1)} fusion(f32[128,4,6]{0,2,1:T(8,128)S(1)} %get-tuple-element.82, f32[128,4,1018]{0,2,1:T(8,128)S(1)} %get-tuple-element.84, f32[128]{0:T(128)} %get-tuple-element.147, f32[128]{0:T(128)} %get-tuple-element.148, f32[128,4,1018]{0,2,1:T(8,128)S(1)} %get-tuple-element.83, ...), kind=kLoop, calls=%fused_computation.161 | loop fusion | flops 15204352 | bytes 16781824 | tf_op jit(solution)/shard_map/stack | solution.py:49
  119.1 4.1 %copy.56 = bf16[256,4096]{1,0:T(8,128)(2,1)} copy(bf16[256,4096]{0,1:T(8,128)(2,1)} %bitcast.200) | data formatting | bytes 4194304
  123.5 4.0 %fusion.72 = f32[4,128,256,1]{2,1,0,3:T(8,128)S(1)} fusion(bf16[256,4,1024]{2,0,1:T(8,128)(2,1)} %all-gather.5.cloned.1.call-done, bf16[1,128,4,1024]{1,3,0,2:T(8,128)(2,1)} %fusion.75, bf16[1,128,4,1024]{1,3,0,2:T(8,128)(2,1)} %copy-done.54, bf16[1,128,4,1024]{1,3,0,2:T(8,128)(2,1)} %copy-done.53, bf16[1,128,4,1024]{1,3,0,2:T(8,128)(2,1)S(1)} %bitcast.198), kind=kOutput, calls=%fused_computation.144 | convolution fusion | flops 1080033280 | bytes 6815744 | tf_op jit(solution)/shard_map/bchw,ohw->bco/dot_general | solution.py:60
  137.3 4.7 %fusion.45 = (f32[128]{0:T(128)}, f32[128]{0:T(128)}, f32[128]{0:T(128)}, f32[128]{0:T(128)}, f32[128]{0:T(128)}, /*index=5*/f32[128]{0:T(128)}, f32[128]{0:T(128)}, f32[128]{0:T(128)}) fusion(bf16[128,4,1024]{0,2,1:T(8,128)(2,1)S(1)} %copy.35, bf16[4,128,4,1024]{1,3,2,0:T(8,128)(2,1)S(1)} %convolution_convert_fusion, f32[128,4,6]{0,2,1:T(8,128)S(1)} %copy-done.77, ...), kind=kLoop, calls=%fused_computation.81 | loop fusion | flops 13630464 | bytes 13635584 | tf_op jit(solution)/shard_map/reduce_sum | solution.py:78
  142.2 3.8 %fusion.48 = (f32[128]{0:T(128)S(1)}, f32[128]{0:T(128)S(1)}, f32[128]{0:T(128)S(1)}, f32[128]{0:T(128)S(1)}, f32[128]{0:T(128)S(1)}, /*index=5*/f32[128]{0:T(128)S(1)}, f32[128]{0:T(128)S(1)}) fusion(bf16[128,2,1024]{0,2,1:T(8,128)(2,1)S(1)} %copy-done.39, bf16[128,2,1024]{0,2,1:T(8,128)(2,1)} %collective-permute-done.2, ...), kind=kLoop, calls=%fused_computation.84 | loop fusion | flops 13630592 | bytes 13635072 | tf_op jit(solution)/shard_map/reduce_sum | solution.py:78
  146.2 6.4 %fusion.49 = (f32[128]{0:T(128)S(1)}, f32[128]{0:T(128)S(1)}, f32[128]{0:T(128)S(1)}, f32[128]{0:T(128)S(1)}, f32[128]{0:T(128)S(1)}, /*index=5*/f32[128]{0:T(128)S(1)}) fusion(f32[128,4,6]{0,2,1:T(8,128)S(1)} %copy-done.79, f32[128,4,1018]{0,2,1:T(8,128)} %copy-done.12, bf16[4,128,4,1024]{1,3,2,0:T(8,128)(2,1)} %copy-done.2, ...), kind=kLoop, calls=%fused_computation.85 | loop fusion | flops 11009280 | bytes 13634560 | tf_op jit(solution)/shard_map/reduce_sum | solution.py:78
  152.8 3.2 reshape.53
  171.7 3.4 collective-permute-start.16
  175.1 11.5 %collective-permute-done.10 = bf16[128,2,1024]{0,2,1:T(8,128)(2,1)S(1)} collective-permute-done((bf16[128,2,1024]{0,2,1:T(8,128)(2,1)S(1)}, bf16[128,2,1024]{0,2,1:T(8,128)(2,1)S(1)}, u32[]{:S(2)}, u32[]{:S(2)}) %collective-permute-start.10) | collective-permute-done | bytes 524320 | tf_op jit(solution)/shard_map/ppermute | solution.py:15
  188.6 17.6 %collective-permute-done.11 = bf16[128,2,1024]{0,2,1:T(8,128)(2,1)S(1)} collective-permute-done((bf16[128,2,1024]{0,2,1:T(8,128)(2,1)S(1)}, bf16[128,2,1024]{0,2,1:T(8,128)(2,1)S(1)}, u32[]{:S(2)}, u32[]{:S(2)}) %collective-permute-start.11) | collective-permute-done | bytes 524320 | tf_op jit(solution)/shard_map/ppermute | solution.py:15
  212.3 30.9 %collective-permute-start.14 = (bf16[128,4,1024]{0,2,1:T(8,128)(2,1)S(1)}, bf16[128,4,1024]{0,2,1:T(8,128)(2,1)S(1)}, u32[]{:S(2)}, u32[]{:S(2)}) collective-permute-start(bf16[128,4,1024]{0,2,1:T(8,128)(2,1)S(1)} %get-tuple-element.47), channel_id=1, source_target_pairs={{6,0},{8,2},{10,4},{12,6},{14,8},{16,10},{18,12},{20,14},{22,16},{... | collective-permute-start | bytes 3145736 | tf_op jit(solution)/shard_map/ppermute | solution.py:15
  247.9 11.1 %collective-permute-done.13 = bf16[128,2,1024]{0,2,1:T(8,128)(2,1)S(1)} collective-permute-done((bf16[128,2,1024]{0,2,1:T(8,128)(2,1)S(1)}, bf16[128,2,1024]{0,2,1:T(8,128)(2,1)S(1)}, u32[]{:S(2)}, u32[]{:S(2)}) %collective-permute-start.13) | collective-permute-done | bytes 524320 | tf_op jit(solution)/shard_map/ppermute | solution.py:15
  260.4 26.6 %collective-permute-done.15 = bf16[128,4,1024]{0,2,1:T(8,128)(2,1)S(1)} collective-permute-done((bf16[128,4,1024]{0,2,1:T(8,128)(2,1)S(1)}, bf16[128,4,1024]{0,2,1:T(8,128)(2,1)S(1)}, u32[]{:S(2)}, u32[]{:S(2)}) %collective-permute-start.15) | collective-permute-done | bytes 1048608 | tf_op jit(solution)/shard_map/ppermute | solution.py:15
  293.2 15.8 %fusion.40 = f32[128,4,1024]{0,2,1:T(8,128)} fusion(f32[128,4,6]{0,2,1:T(8,128)S(1)} %get-tuple-element.74, f32[128,4,1018]{0,2,1:T(8,128)S(1)} %get-tuple-element.76, f32[128,4,1018]{0,2,1:T(8,128)S(1)} %get-tuple-element.75, f32[128,4,6]{0,2,1:T(8,128)S(1)} %get-tuple-element.73, f32[128,4,6]{0,2,1:T(8,128)S(1)} %get-tuple-element.70, ...), kind=kLoop, calls=%fused_computation.76 | loop fusion | flops 45088768 | bytes 50345472 | tf_op jit(solution)/shard_map/add | solution.py:74
  309.0 3.0 copy.47
  315.4 41.2 %reduce_sum.279 = f32[134528]{0:T(1024)S(1)} reduce(f32[16,1,134528]{2,1,0:T(1,128)} %all-gather.7.cloned.1.call-done, f32[]{:T(128)} %constant.2.clone.1), dimensions={0,1}, to_apply=%region_28.29 | reduce | flops 2017920 | bytes 9147908 | tf_op jit(solution)/shard_map/reduce_sum | solution.py:87
  (349 shorter events, 89.1 us)
Async XLA Ops:
  7.2 109.4 %copy-start = (bf16[4,128,256]{2,1,0:T(8,128)(2,1)S(1)}, bf16[4,128,256]{2,1,0:T(8,128)(2,1)}, u32[]{:S(2)}) copy-start(bf16[4,128,256]{2,1,0:T(8,128)(2,1)} %param.6) | copy-start | bytes 786436
  7.2 116.3 %all-gather.5.cloned.1.call-start = ((), (), s32[]{:S(2)}) async-start(), calls=%async_computation.1 | async-start | bytes 3145728 | tf_op jit(solution)/shard_map/all_gather | solution.py:58
  10.3 55.3 %collective-permute-start.8 = (bf16[128,2,1024]{0,2,1:T(8,128)(2,1)}, bf16[128,2,1024]{0,2,1:T(8,128)(2,1)}, u32[]{:S(2)}, u32[]{:S(2)}) collective-permute-start(bf16[128,2,1024]{0,2,1:T(8,128)(2,1)} %get-tuple-element.125), channel_id=1, source_target_pairs={{8,0},{10,2},{12,4},{14,6},{16,8},{18,10},{20,12},{22,14},{24,16},... | collective-permute-start | bytes 1572872 | tf_op jit(solution)/shard_map/ppermute | solution.py:15
  12.7 17.8 %collective-permute-start.6 = (bf16[128,2,1024]{0,2,1:T(8,128)(2,1)}, bf16[128,2,1024]{0,2,1:T(8,128)(2,1)S(1)}, u32[]{:S(2)}, u32[]{:S(2)}) collective-permute-start(bf16[128,2,1024]{0,2,1:T(8,128)(2,1)} %get-tuple-element.125), channel_id=1, source_target_pairs={{0,10},{2,12},{4,14},{6,16},{8,18},{10,20},{12,22},{14,24},{16,26}... | collective-permute-start | bytes 1572872 | tf_op jit(solution)/shard_map/ppermute | solution.py:15
  16.1 59.1 %collective-permute-start.2 = (bf16[128,2,1024]{0,2,1:T(8,128)(2,1)}, bf16[128,2,1024]{0,2,1:T(8,128)(2,1)}, u32[]{:S(2)}, u32[]{:S(2)}) collective-permute-start(bf16[128,2,1024]{0,2,1:T(8,128)(2,1)} %get-tuple-element.125), channel_id=1, source_target_pairs={{2,0},{4,2},{6,4},{8,6},{10,8},{12,10},{14,12},{16,14},{18,16},{20... | collective-permute-start | bytes 1572872 | tf_op jit(solution)/shard_map/ppermute | solution.py:15
  20.1 61.3 %collective-permute-start = (bf16[128,2,1024]{0,2,1:T(8,128)(2,1)}, bf16[128,2,1024]{0,2,1:T(8,128)(2,1)}, u32[]{:S(2)}, u32[]{:S(2)}) collective-permute-start(bf16[128,2,1024]{0,2,1:T(8,128)(2,1)} %get-tuple-element.125), channel_id=1, source_target_pairs={{0,4},{2,6},{4,8},{6,10},{8,12},{10,14},{12,16},{14,18},{16,20},{1... | collective-permute-start | bytes 1572872 | tf_op jit(solution)/shard_map/ppermute | solution.py:15
  23.4 288.6 %reduce-scatter.4.cloned.1.call-start = ((), (), s32[]{:S(2)}) async-start(), calls=%async_computation.3 | async-start | bytes 3145728
  23.5 36.7 %collective-permute-start.7 = (bf16[128,2,1024]{0,2,1:T(8,128)(2,1)}, bf16[128,2,1024]{0,2,1:T(8,128)(2,1)S(1)}, u32[]{:S(2)}, u32[]{:S(2)}) collective-permute-start(bf16[128,2,1024]{0,2,1:T(8,128)(2,1)} %get-tuple-element.126), channel_id=1, source_target_pairs={{0,8},{2,10},{4,12},{6,14},{8,16},{10,18},{12,20},{14,22},{16,24},... | collective-permute-start | bytes 1572872 | tf_op jit(solution)/shard_map/ppermute | solution.py:15
  30.4 38.5 %collective-permute-start.9 = (bf16[128,2,1024]{0,2,1:T(8,128)(2,1)}, bf16[128,2,1024]{0,2,1:T(8,128)(2,1)S(1)}, u32[]{:S(2)}, u32[]{:S(2)}) collective-permute-start(bf16[128,2,1024]{0,2,1:T(8,128)(2,1)} %get-tuple-element.126), channel_id=1, source_target_pairs={{10,0},{12,2},{14,4},{16,6},{18,8},{20,10},{22,12},{24,14},{26,16}... | collective-permute-start | bytes 1572872 | tf_op jit(solution)/shard_map/ppermute | solution.py:15
  60.1 19.5 %collective-permute-start.3 = (bf16[128,2,1024]{0,2,1:T(8,128)(2,1)}, bf16[128,2,1024]{0,2,1:T(8,128)(2,1)S(1)}, u32[]{:S(2)}, u32[]{:S(2)}) collective-permute-start(bf16[128,2,1024]{0,2,1:T(8,128)(2,1)} %get-tuple-element.126), channel_id=1, source_target_pairs={{4,0},{6,2},{8,4},{10,6},{12,8},{14,10},{16,12},{18,14},{20,16},{2... | collective-permute-start | bytes 1572872 | tf_op jit(solution)/shard_map/ppermute | solution.py:15
  65.6 30.7 %collective-permute-start.1 = (bf16[128,2,1024]{0,2,1:T(8,128)(2,1)}, bf16[128,2,1024]{0,2,1:T(8,128)(2,1)S(1)}, u32[]{:S(2)}, u32[]{:S(2)}) collective-permute-start(bf16[128,2,1024]{0,2,1:T(8,128)(2,1)} %get-tuple-element.126), channel_id=1, source_target_pairs={{0,2},{2,4},{4,6},{6,8},{8,10},{10,12},{12,14},{14,16},{16,18},{18... | collective-permute-start | bytes 1572872 | tf_op jit(solution)/shard_map/ppermute | solution.py:15
  68.9 42.9 %collective-permute-start.5 = (bf16[128,4,1024]{0,2,1:T(8,128)(2,1)S(1)}, bf16[128,4,1024]{0,2,1:T(8,128)(2,1)S(1)}, u32[]{:S(2)}, u32[]{:S(2)}) collective-permute-start(bf16[128,4,1024]{0,2,1:T(8,128)(2,1)S(1)} %copy.35), channel_id=1, source_target_pairs={{6,0},{8,2},{10,4},{12,6},{14,8},{16,10},{18,12},{20,14},{22,16},{... | collective-permute-start | bytes 3145736 | tf_op jit(solution)/shard_map/ppermute | solution.py:15
  75.2 36.7 %collective-permute-start.4 = (bf16[128,4,1024]{0,2,1:T(8,128)(2,1)S(1)}, bf16[128,4,1024]{0,2,1:T(8,128)(2,1)S(1)}, u32[]{:S(2)}, u32[]{:S(2)}) collective-permute-start(bf16[128,4,1024]{0,2,1:T(8,128)(2,1)S(1)} %copy.35), channel_id=1, source_target_pairs={{0,6},{2,8},{4,10},{6,12},{8,14},{10,16},{12,18},{14,20},{16,22},{... | collective-permute-start | bytes 3145736 | tf_op jit(solution)/shard_map/ppermute | solution.py:15
  123.2 192.2 %all-gather.7.cloned.1.call-start = ((), (), s32[]{:S(2)}) async-start(), calls=%async_computation.2 | async-start | bytes 9147904 | tf_op jit(solution)/shard_map/all_gather | solution.py:86
  158.9 51.3 %collective-permute-start.17 = (bf16[128,2,1024]{0,2,1:T(8,128)(2,1)S(1)}, bf16[128,2,1024]{0,2,1:T(8,128)(2,1)S(1)}, u32[]{:S(2)}, u32[]{:S(2)}) collective-permute-start(bf16[128,2,1024]{0,2,1:T(8,128)(2,1)S(1)} %get-tuple-element.94), channel_id=1, source_target_pairs={{10,0},{12,2},{14,4},{16,6},{18,8},{20,10},{22,12},{24,14},{26,16}... | collective-permute-start | bytes 1572872 | tf_op jit(solution)/shard_map/ppermute | solution.py:15
  160.9 25.7 %collective-permute-start.10 = (bf16[128,2,1024]{0,2,1:T(8,128)(2,1)S(1)}, bf16[128,2,1024]{0,2,1:T(8,128)(2,1)S(1)}, u32[]{:S(2)}, u32[]{:S(2)}) collective-permute-start(bf16[128,2,1024]{0,2,1:T(8,128)(2,1)S(1)} %get-tuple-element.103), channel_id=1, source_target_pairs={{2,0},{4,2},{6,4},{8,6},{10,8},{12,10},{14,12},{16,14},{18,16},{20... | collective-permute-start | bytes 1572872 | tf_op jit(solution)/shard_map/ppermute | solution.py:15
  162.8 43.4 %collective-permute-start.11 = (bf16[128,2,1024]{0,2,1:T(8,128)(2,1)S(1)}, bf16[128,2,1024]{0,2,1:T(8,128)(2,1)S(1)}, u32[]{:S(2)}, u32[]{:S(2)}) collective-permute-start(bf16[128,2,1024]{0,2,1:T(8,128)(2,1)S(1)} %get-tuple-element.104), channel_id=1, source_target_pairs={{4,0},{6,2},{8,4},{10,6},{12,8},{14,10},{16,12},{18,14},{20,16},{2... | collective-permute-start | bytes 1572872 | tf_op jit(solution)/shard_map/ppermute | solution.py:15
  169.1 43.2 %collective-permute-start.18 = (bf16[128,2,1024]{0,2,1:T(8,128)(2,1)S(1)}, bf16[128,2,1024]{0,2,1:T(8,128)(2,1)S(1)}, u32[]{:S(2)}, u32[]{:S(2)}) collective-permute-start(bf16[128,2,1024]{0,2,1:T(8,128)(2,1)S(1)} %get-tuple-element.93), channel_id=1, source_target_pairs={{0,10},{2,12},{4,14},{6,16},{8,18},{10,20},{12,22},{14,24},{16,26}... | collective-permute-start | bytes 1572872 | tf_op jit(solution)/shard_map/ppermute | solution.py:15
  171.7 36.6 %collective-permute-start.16 = (bf16[128,2,1024]{0,2,1:T(8,128)(2,1)S(1)}, bf16[128,2,1024]{0,2,1:T(8,128)(2,1)S(1)}, u32[]{:S(2)}, u32[]{:S(2)}) collective-permute-start(bf16[128,2,1024]{0,2,1:T(8,128)(2,1)S(1)} %get-tuple-element.93), channel_id=1, source_target_pairs={{8,0},{10,2},{12,4},{14,6},{16,8},{18,10},{20,12},{22,14},{24,16},... | collective-permute-start | bytes 1572872 | tf_op jit(solution)/shard_map/ppermute | solution.py:15
  186.6 56.6 %collective-permute-start.19 = (bf16[128,2,1024]{0,2,1:T(8,128)(2,1)S(1)}, bf16[128,2,1024]{0,2,1:T(8,128)(2,1)S(1)}, u32[]{:S(2)}, u32[]{:S(2)}) collective-permute-start(bf16[128,2,1024]{0,2,1:T(8,128)(2,1)S(1)} %get-tuple-element.94), channel_id=1, source_target_pairs={{0,8},{2,10},{4,12},{6,14},{8,16},{10,18},{12,20},{14,22},{16,24},... | collective-permute-start | bytes 1572872 | tf_op jit(solution)/shard_map/ppermute | solution.py:15
  206.2 41.7 %collective-permute-start.12 = (bf16[128,2,1024]{0,2,1:T(8,128)(2,1)S(1)}, bf16[128,2,1024]{0,2,1:T(8,128)(2,1)S(1)}, u32[]{:S(2)}, u32[]{:S(2)}) collective-permute-start(bf16[128,2,1024]{0,2,1:T(8,128)(2,1)S(1)} %get-tuple-element.103), channel_id=1, source_target_pairs={{0,4},{2,6},{4,8},{6,10},{8,12},{10,14},{12,16},{14,18},{16,20},{1... | collective-permute-start | bytes 1572872 | tf_op jit(solution)/shard_map/ppermute | solution.py:15
  208.3 50.7 %collective-permute-start.13 = (bf16[128,2,1024]{0,2,1:T(8,128)(2,1)S(1)}, bf16[128,2,1024]{0,2,1:T(8,128)(2,1)S(1)}, u32[]{:S(2)}, u32[]{:S(2)}) collective-permute-start(bf16[128,2,1024]{0,2,1:T(8,128)(2,1)S(1)} %get-tuple-element.104), channel_id=1, source_target_pairs={{0,2},{2,4},{4,6},{6,8},{8,10},{10,12},{12,14},{14,16},{16,18},{18... | collective-permute-start | bytes 1572872 | tf_op jit(solution)/shard_map/ppermute | solution.py:15
  210.2 76.8 %collective-permute-start.15 = (bf16[128,4,1024]{0,2,1:T(8,128)(2,1)S(1)}, bf16[128,4,1024]{0,2,1:T(8,128)(2,1)S(1)}, u32[]{:S(2)}, u32[]{:S(2)}) collective-permute-start(bf16[128,4,1024]{0,2,1:T(8,128)(2,1)S(1)} %get-tuple-element.47), channel_id=1, source_target_pairs={{0,6},{2,8},{4,10},{6,12},{8,14},{10,16},{12,18},{14,20},{16,22},{... | collective-permute-start | bytes 3145736 | tf_op jit(solution)/shard_map/ppermute | solution.py:15
  212.3 74.7 %collective-permute-start.14 = (bf16[128,4,1024]{0,2,1:T(8,128)(2,1)S(1)}, bf16[128,4,1024]{0,2,1:T(8,128)(2,1)S(1)}, u32[]{:S(2)}, u32[]{:S(2)}) collective-permute-start(bf16[128,4,1024]{0,2,1:T(8,128)(2,1)S(1)} %get-tuple-element.47), channel_id=1, source_target_pairs={{6,0},{8,2},{10,4},{12,6},{14,8},{16,10},{18,12},{20,14},{22,16},{... | collective-permute-start | bytes 3145736 | tf_op jit(solution)/shard_map/ppermute | solution.py:15
  (120 other events, 2290.2 us)
Sparse Core Ops, SparseCore 0:
  23.5 34.5 all-gather.4
  123.3 31.9 reduce-scatter.3
  157.6 120.4 all-gather.6
